TPU v7x, 256 devices: a whole 4x4x8 slice. The times are simulated.
256 devices in a mesh: row: 32 (over x, y, core), col: 8 (over z).
Axes of the slice: x: 4, y: 4, z: 8, core: 2. Of those that a mesh axis runs over, the one named last changes fastest.
Arguments:
- features: bfloat16 [8192, 1024], P('row', 'col'), may hold values from -6 to 6
- grad_out: bfloat16 [8192, 1024], P('row', 'col'), may hold values from -6 to 6
- weight: bfloat16 [1024, 1024], replicated, may hold values from -0.1875 to 0.1875
- root_weight: bfloat16 [1024, 1024], replicated, may hold values from -0.1875 to 0.1875
- values: bfloat16 [32, 8, 8, 128, 128], P('row', 'col'), may hold values from -0.125 to 0.125
- positions: int32 [32, 8, 8], P('row', 'col'), may hold values from 0 to 15, as said below
- counts: int32 [32, 8], P('row', 'col'), may hold values from 1 to 8, as said below
Outputs:
- activations: bfloat16 [8192, 1024], P('row', 'col')
- feature_grad: float32 [8192, 1024], P('row', 'col')
- weight_grad: float32 [1024, 1024], P('col')
- root_grad: float32 [1024, 1024], P('col')
Inputs may be any that keep to these rules, and one draw needn't show every extreme that they name: Within the first counts slots of a tile the positions are distinct; position p is block row p // 8 and block column p % 8 of the tile. `counts`: some tile uses all 8 slots in every draw; about a quarter of the block rows have much fuller tiles (4 or 8 used slots) than the rest (1 or 2).
All inputs are finite; a program needn't handle non-finite values.
Results may differ from a plain program's by a relative error of at most 0.012.
Values may be sent and summed in bfloat16 or wider, within the bound.
No kernel may reach another device: no remote copies, remote signals or barrier semaphores. Data moves between devices by JAX's collectives and lax.ppermute only.
A program may use at most 64 MiB of HBM per device.

v0:
```python
import math
import jax
import jax.numpy as jnp
from jax import lax
from jax.sharding import PartitionSpec as P


def silu_grad(preact):
    sig = jax.nn.sigmoid(preact)
    return sig * (1.0 + preact * (1.0 - sig))


def gather_rows(block, axis_name, parts):
    spread = jnp.broadcast_to(block[None], (parts,) + block.shape)
    got = lax.all_to_all(spread, axis_name, 0, 0, tiled=True)
    return got.reshape((parts * block.shape[0],) + block.shape[1:])


def reduce_rows(block, axis_name, parts):
    pieces = block.reshape((parts, block.shape[0] // parts) + block.shape[1:])
    got = lax.all_to_all(pieces, axis_name, 0, 0, tiled=True)
    return got.astype(jnp.float32).sum(0)


def per_device(features, grad_out, weight, root_weight, values, positions, counts):
    node_rows, feat_dev = features.shape
    slots, block_edge = (values.shape[2], values.shape[-1])
    row_blocks = node_rows // block_edge
    col_count = lax.axis_size("col")
    row_count = lax.axis_size("row")
    col_index = lax.axis_index("col")
    live = (jnp.arange(slots, dtype=jnp.int32) < counts[0, 0]).astype(values.dtype)
    own_vals = (values[0, 0] * live[:, None, None]).reshape(slots * block_edge, block_edge)
    pos_row = jnp.zeros((block_edge, block_edge), values.dtype)
    pos_row = lax.dynamic_update_slice(
        pos_row, positions[0, 0].astype(values.dtype).reshape(1, slots), (0, 0)
    )
    packed = jnp.concatenate([own_vals, pos_row, features, grad_out], axis=0)
    all_packed = lax.all_gather(packed, "col", axis=0, tiled=True).reshape(
        col_count, packed.shape[0], block_edge
    )
    tile_vals = all_packed.reshape(col_count, -1, block_edge, block_edge)[:, :slots]
    tile_pos = all_packed[:, slots * block_edge, :slots].astype(jnp.int32)
    cb = row_count * node_rows // col_count // block_edge
    n_pos = row_blocks * cb
    onehot = (tile_pos[:, :, None] == jnp.arange(n_pos, dtype=jnp.int32)[None, None, :]).astype(
        values.dtype
    )
    dense = jnp.einsum(
        "tsp,tsij->tpij", onehot, tile_vals, preferred_element_type=jnp.float32
    ).astype(values.dtype)
    dense = dense.reshape(col_count, row_blocks, cb, block_edge, block_edge)
    x_all = gather_rows(features, "row", row_count)
    x_tiles = x_all.reshape(col_count, cb, block_edge, feat_dev)
    col_hot = (
        (tile_pos % cb)[:, :, None] == jnp.arange(cb, dtype=jnp.int32)[None, None, :]
    ).astype(values.dtype)
    row_hot = (
        (tile_pos // cb)[:, :, None] == jnp.arange(row_blocks, dtype=jnp.int32)[None, None, :]
    ).astype(jnp.float32)
    chosen = jnp.einsum(
        "tsc,tcjf->tsjf", col_hot, x_tiles, preferred_element_type=jnp.float32
    ).astype(values.dtype)
    products = jnp.einsum("tsij,tsjf->tsif", tile_vals, chosen, preferred_element_type=jnp.float32)
    agg_f32 = jnp.sum(products[:, :, None] * row_hot[:, :, :, None, None], axis=(0, 1))
    aggregated = agg_f32.reshape(node_rows, feat_dev).astype(jnp.bfloat16)
    agg_parts = gather_rows(aggregated, "col", col_count).reshape(col_count, node_rows, feat_dev)
    nodes = row_count * node_rows
    dense_t = jnp.transpose(dense, (0, 2, 4, 1, 3)).reshape(nodes, node_rows)
    agg_parts, dense_t = lax.optimization_barrier((agg_parts, dense_t))
    agg_full = jnp.moveaxis(agg_parts, 0, 1).reshape(node_rows, col_count * feat_dev)
    pair_parts = all_packed[:, (slots + 1) * block_edge :].reshape(
        col_count, 2, node_rows, feat_dev
    )
    pair_full = jnp.moveaxis(pair_parts, 0, 2).reshape(2, node_rows, col_count * feat_dev)
    feat_full = pair_full[0]
    grad_full = pair_full[1]
    preact = jnp.dot(agg_full, weight, preferred_element_type=jnp.float32) + jnp.dot(
        feat_full, root_weight, preferred_element_type=jnp.float32
    )
    preact_own = lax.dynamic_slice_in_dim(preact, col_index * feat_dev, feat_dev, 1)
    activations = jax.nn.silu(preact_own).astype(jnp.bfloat16)
    preact_grad = (grad_full.astype(jnp.float32) * silu_grad(preact)).astype(jnp.bfloat16)
    contract_rows = (((0,), (0,)), ((), ()))
    weight_part = lax.dot_general(
        aggregated, preact_grad, contract_rows, preferred_element_type=jnp.float32
    )
    root_part = lax.dot_general(
        features, preact_grad, contract_rows, preferred_element_type=jnp.float32
    )
    grad_scale = 1.0 / math.sqrt(nodes)
    both = jnp.concatenate([weight_part, root_part], axis=0) * grad_scale
    sum_rows = both.shape[0] // row_count
    lane_tiles = both.shape[1] // block_edge
    sum_lanes = sum_rows * lane_tiles
    both_tiled = (
        both.astype(jnp.bfloat16)
        .reshape(row_count, sum_rows, lane_tiles, block_edge)
        .transpose(0, 2, 1, 3)
        .reshape(row_count * sum_lanes, block_edge)
    )
    sum_pair = reduce_rows(both_tiled, "row", row_count).astype(jnp.bfloat16)
    w_rows = lax.dynamic_slice_in_dim(weight, col_index * feat_dev, feat_dev, 0)
    r_rows = lax.dynamic_slice_in_dim(root_weight, col_index * feat_dev, feat_dev, 0)
    contract_cols = (((1,), (1,)), ((), ()))
    aggregated_grad = lax.dot_general(
        preact_grad, w_rows, contract_cols, preferred_element_type=jnp.float32
    ).astype(jnp.bfloat16)
    own_grad = lax.dot_general(
        preact_grad, r_rows, contract_cols, preferred_element_type=jnp.float32
    )
    column_terms = jnp.dot(dense_t, aggregated_grad, preferred_element_type=jnp.float32)
    term_pieces = column_terms.astype(jnp.bfloat16).reshape(row_count, node_rows, feat_dev)
    room = jnp.zeros((row_count,) + sum_pair.shape, term_pieces.dtype)
    outgoing = jnp.concatenate([term_pieces, room], axis=1)
    outgoing, own_grad = lax.optimization_barrier((outgoing, own_grad))
    outgoing = lax.dynamic_update_slice(
        outgoing, jnp.broadcast_to(sum_pair[None], room.shape), (0, node_rows, 0)
    )
    incoming = lax.all_to_all(outgoing, "row", 0, 0, tiled=True)
    summed_cols = incoming[:, :node_rows].astype(jnp.float32).sum(0)
    got_sums = (
        incoming[:, node_rows:]
        .reshape(row_count, lane_tiles, sum_rows, block_edge)
        .transpose(0, 2, 1, 3)
        .astype(jnp.float32)
    )
    half = row_count // 2
    weight_sum = got_sums[:half].reshape(feat_dev, -1)
    root_sum = got_sums[half:].reshape(feat_dev, -1)
    feature_grad = summed_cols + own_grad
    return (activations, feature_grad, weight_sum, root_sum)


def solution(mesh):
    in_specs = (
        P("row", "col"),
        P("row", "col"),
        P(),
        P(),
        P("row", "col", None, None, None),
        P("row", "col", None),
        P("row", "col"),
    )
    out_specs = (P("row", "col"), P("row", "col"), P("col", None), P("col", None))
    return jax.shard_map(
        per_device, mesh=mesh, in_specs=in_specs, out_specs=out_specs, check_vma=False
    )
```

profile of v0, /device:TPU:1, one launch (start us, length us, event | category | flops | bytes accessed | tf_op | source)
XLA Modules:
  0.0 168.5 jit_solution(12683011915921730170)
XLA Ops:
  7.2 0.0 copy-start
  7.2 0.0 all-gather.2.cloned.1.call-start
  7.2 0.8 convert_bitcast_fusion.2
  8.7 0.1 broadcast_bitcast_fusion
  8.8 1.1 bitcast_multiply_fusion.1
  9.9 1.7 fusion.17
  11.6 0.0 all-gather.2.cloned.1.call-update
  11.6 2.6 %broadcast_in_dim.6 = bf16[32,256,128]{2,1,0:T(8,128)(2,1)} broadcast(bf16[256,128]{1,0:T(8,128)(2,1)} %param.7), dimensions={1,2} | broadcast | bytes 2162688 | tf_op jit(solution)/shard_map/broadcast_in_dim | solution.py:14
  14.2 8.6 %all-to-all-start = ((bf16[32,256,128]{2,1,0:T(8,128)(2,1)}), bf16[32,256,128]{2,1,0:T(8,128)(2,1)}, u32[]{:S(2)}, u32[]{:S(2)}) async-start(bf16[32,256,128]{2,1,0:T(8,128)(2,1)} %broadcast_in_dim.6), calls=%async_computation | async-start | bytes 4194304 | tf_op jit(solution)/shard_map/all_to_all | solution.py:15
  22.9 39.9 %all-gather.2.cloned.1.call-done = bf16[13312,128]{1,0:T(8,128)(2,1)} async-done(((bf16[1664,128]{1,0:T(8,128)(2,1)}), bf16[13312,128]{1,0:T(8,128)(2,1)}) %all-gather.2.cloned.1.call-update) | async-done | bytes 3407888 | tf_op jit(solution)/shard_map/all_gather | solution.py:39
  62.8 0.7 slice_convert_fusion.1
  63.5 0.1 fusion.24
  63.6 0.0 all-to-all-done
  63.6 0.0 copy-start.1
  63.6 3.1 %fusion.5 = bf16[8,8,128,128]{3,1,2,0:T(8,128)(2,1)S(1)} fusion(bf16[8,8,128,128]{3,2,1,0:T(8,128)(2,1)} %bitcast.9, s32[8,8]{1,0:T(8,128)S(1)} %get-tuple-element.16), kind=kOutput, calls=%fused_computation.10 | convolution fusion | flops 17826304 | bytes 4194560 | tf_op jit(solution)/shard_map/tsc,tcjf->tsjf/dot_general | solution.py:61
  66.7 0.7 fusion.1
  67.4 0.7 multiply_reduce_fusion
  68.1 0.1 copy.22
  68.2 0.8 broadcast_in_dim.7
  69.1 4.2 %all-to-all-start.1 = ((bf16[8,256,128]{1,2,0:T(8,128)(2,1)}), bf16[8,256,128]{1,2,0:T(8,128)(2,1)}, u32[]{:S(2)}, u32[]{:S(2)}) async-start(bf16[8,256,128]{1,2,0:T(8,128)(2,1)} %broadcast_in_dim.7), calls=%async_computation.1 | async-start | bytes 1048576 | tf_op jit(solution)/shard_map/all_to_all | solution.py:15
  73.2 1.3 slice.40
  74.6 1.8 %slice.39 = bf16[8,8,128,128]{3,2,1,0:T(8,128)(2,1)S(1)} slice(bf16[8,13,128,128]{3,2,1,0:T(8,128)(2,1)} %bitcast.89), slice={[0:8], [0:8], [0:128], [0:128]} | slice | bytes 4194304 | tf_op jit(solution)/shard_map/slice | solution.py:42
  76.4 0.7 copy.48
  77.1 1.9 %convert_bitcast_fusion = bf16[8,2,8,128,128]{4,2,1,3,0:T(8,128)(2,1)S(1)} fusion(bf16[8,8,128,128]{3,2,1,0:T(8,128)(2,1)S(1)} %slice.39, s32[8,8]{1,0:T(8,128)S(1)} %bitcast.96), kind=kOutput, calls=%fused_computation.4 | convolution fusion | flops 35652608 | bytes 6291712 | tf_op jit(solution)/shard_map/tsp,tsij->tpij/dot_general | solution.py:49
  79.0 3.2 %copy.47 = bf16[8,2,8,128,128]{4,2,0,3,1:T(8,128)(2,1)} copy(bf16[8,2,8,128,128]{4,2,1,3,0:T(8,128)(2,1)S(1)} %convert_bitcast_fusion) | data formatting | bytes 8388608 | tf_op jit(solution)/shard_map/reshape | solution.py:52
  82.1 7.3 %reshape.122 = bf16[8192,256]{0,1:T(8,128)(2,1)} reshape(bf16[8,8,128,2,128]{2,1,0,4,3:T(8,128)(2,1)} %bitcast.83) | data formatting | bytes 8388608 | tf_op jit(solution)/shard_map/reshape | solution.py:69
  89.4 1.2 slice_convert_fusion
  90.7 0.5 all-to-all-done.1
  91.2 1.9 %fusion.34 = f32[256,1024]{1,0:T(8,128)S(1)} fusion(bf16[256,1024]{0,1:T(8,128)(2,1)} %bitcast.16, bf16[1024,1024]{1,0:T(8,128)(2,1)S(1)} %copy-done), kind=kOutput, calls=%fused_computation.62 | convolution fusion | flops 536870912 | bytes 3670016 | tf_op jit(solution)/shard_map/dot_general | solution.py:78
  93.1 0.3 copy-done.5
  93.4 2.1 %fusion.8 = (bf16[256,1024]{1,0:T(8,128)(2,1)S(1)}, f32[256,1024]{1,0:T(8,128)}) fusion(f32[32,8,8,128]{3,2,1,0:T(8,128)S(1)} %bitcast.91, f32[256,1024]{1,0:T(8,128)S(1)} %fusion.34, bf16[1024,1024]{1,0:T(8,128)(2,1)S(1)} %copy-done.5, bf16[32,8,8,128]{3,2,1,0:T(8,128)(2,1)S(1)} %bitcast.94), kind=kOutput, calls=%fused_computation.17 | convolution fusion | flops 539492352 | bytes 6291456 | tf_op jit(solution)/shard_map/dot_general | solution.py:78
  95.5 0.3 convolution_bitcast_fusion
  95.8 0.2 fusion.35
  96.0 0.9 fusion.12
  97.0 7.4 %all-to-all-start.2 = ((bf16[32,64,128]{2,1,0:T(8,128)(2,1)}), bf16[32,64,128]{2,1,0:T(8,128)(2,1)S(1)}, u32[]{:S(2)}, u32[]{:S(2)}) async-start(bf16[32,64,128]{2,1,0:T(8,128)(2,1)} %fusion.12), calls=%async_computation.2 | async-start | bytes 1048576 | tf_op jit(solution)/shard_map/all_to_all | solution.py:21
  104.3 5.3 %convolution_convert_fusion = bf16[8192,128]{1,0:T(8,128)(2,1)} fusion(bf16[8192,256]{0,1:T(8,128)(2,1)} %reshape.122, bf16[256,1024]{1,0:T(8,128)(2,1)S(1)} %get-tuple-element.18, bf16[1024,1024]{1,0:T(8,128)(2,1)S(1)} %copy-done, s32[]{:T(128)S(6)} %select_n.27), kind=kOutput, calls=%fused_computation | convolution fusion | flops 605061120 | bytes 7077892 | tf_op jit(solution)/shard_map/dot_general | solution.py:112
  109.7 3.5 %concatenate.10 = bf16[32,320,128]{2,1,0:T(8,128)(2,1)} pad(bf16[32,256,128]{2,1,0:T(8,128)(2,1)} %bitcast.84, bf16[]{:T(256)} %constant.37.clone.1), padding=0_0x0_64x0_0 | pad | bytes 4718594 | tf_op jit(solution)/shard_map/concatenate | solution.py:115
  113.1 1.2 fusion.18
  114.4 1.6 all-to-all-done.2
  115.9 0.1 reduce_sum.31
  116.0 1.0 broadcast_dynamic-update-slice_fusion
  117.0 5.9 %all-to-all-start.3 = ((bf16[32,320,128]{2,1,0:T(8,128)(2,1)}), bf16[32,320,128]{2,1,0:T(8,128)(2,1)}, u32[]{:S(2)}, u32[]{:S(2)}) async-start(bf16[32,320,128]{2,1,0:T(8,128)(2,1)} %broadcast_dynamic-update-slice_fusion), calls=%async_computation.3 | async-start | bytes 5242880 | tf_op jit(solution)/shard_map/all_to_all | solution.py:120
  122.9 1.6 multiply_convert_fusion
  124.5 32.4 %all-to-all-done.3 = bf16[32,320,128]{2,1,0:T(8,128)(2,1)} async-done(((bf16[32,320,128]{2,1,0:T(8,128)(2,1)}), bf16[32,320,128]{2,1,0:T(8,128)(2,1)}, u32[]{:S(2)}, u32[]{:S(2)}) %all-to-all-start.3) | async-done | bytes 2621472 | tf_op jit(solution)/shard_map/all_to_all | solution.py:120
  156.9 1.1 convert_bitcast_fusion.1
  158.0 1.1 slice_bitcast_fusion
  159.1 1.9 %convert_reduce_fusion = f32[256,128]{1,0:T(8,128)S(1)} fusion(bf16[32,320,128]{2,1,0:T(8,128)(2,1)} %all-to-all-done.3), kind=kLoop, calls=%fused_computation.3 | loop fusion | flops 2064384 | bytes 2228224 | tf_op jit(solution)/shard_map/reduce_sum | solution.py:121
  161.0 0.7 add.46
  (11 shorter events, 0.0 us)
Async XLA Ops:
  7.2 84.0 %copy-start = (bf16[1024,1024]{1,0:T(8,128)(2,1)S(1)}, bf16[1024,1024]{1,0:T(8,128)(2,1)}, u32[]{:S(2)}) copy-start(bf16[1024,1024]{1,0:T(8,128)(2,1)} %param.9) | copy-start | bytes 6291460
  7.2 55.6 %all-gather.2.cloned.1.call-start = ((), (), s32[]{:S(2)}) async-start(), calls=%async_computation.4 | async-start | bytes 3833856 | tf_op jit(solution)/shard_map/all_gather | solution.py:39
  14.2 49.3 %all-to-all-start = ((bf16[32,256,128]{2,1,0:T(8,128)(2,1)}), bf16[32,256,128]{2,1,0:T(8,128)(2,1)}, u32[]{:S(2)}, u32[]{:S(2)}) async-start(bf16[32,256,128]{2,1,0:T(8,128)(2,1)} %broadcast_in_dim.6), calls=%async_computation | async-start | bytes 4194304 | tf_op jit(solution)/shard_map/all_to_all | solution.py:15
  63.6 3.1 %copy-start.1 = (bf16[13312,128]{1,0:T(8,128)(2,1)S(1)}, bf16[13312,128]{1,0:T(8,128)(2,1)}, u32[]{:S(2)}) copy-start(bf16[13312,128]{1,0:T(8,128)(2,1)} %all-gather.2.cloned.1.call-done) | copy-start | bytes 10223620
  69.1 22.1 %all-to-all-start.1 = ((bf16[8,256,128]{1,2,0:T(8,128)(2,1)}), bf16[8,256,128]{1,2,0:T(8,128)(2,1)}, u32[]{:S(2)}, u32[]{:S(2)}) async-start(bf16[8,256,128]{1,2,0:T(8,128)(2,1)} %broadcast_in_dim.7), calls=%async_computation.1 | async-start | bytes 1048576 | tf_op jit(solution)/shard_map/all_to_all | solution.py:15
  91.2 1.9 %copy-start.2 = (f32[1,256,8,128]{3,2,1,0:T(8,128)S(1)}, f32[1,256,8,128]{3,2,1,0:T(8,128)}, u32[]{:S(2)}) copy-start(f32[1,256,8,128]{3,2,1,0:T(8,128)} %get-tuple-element.14) | copy-start | bytes 3145732
  91.2 1.9 %copy-start.4 = (bf16[1,256,8,128]{3,2,1,0:T(8,128)(2,1)S(1)}, bf16[1,256,8,128]{3,2,1,0:T(8,128)(2,1)}, u32[]{:S(2)}) copy-start(bf16[1,256,8,128]{3,2,1,0:T(8,128)(2,1)} %get-tuple-element.15) | copy-start | bytes 1572868
  91.2 2.2 %copy-start.5 = (bf16[1024,1024]{1,0:T(8,128)(2,1)S(1)}, bf16[1024,1024]{1,0:T(8,128)(2,1)}, u32[]{:S(2)}) copy-start(bf16[1024,1024]{1,0:T(8,128)(2,1)} %param.10) | copy-start | bytes 6291460
  93.4 2.1 %copy-start.3 = (bf16[256,128]{1,0:T(8,128)(2,1)S(1)}, bf16[256,128]{1,0:T(8,128)(2,1)}, u32[]{:S(2)}) copy-start(bf16[256,128]{1,0:T(8,128)(2,1)} %param.7) | copy-start | bytes 196612
  97.0 19.0 %all-to-all-start.2 = ((bf16[32,64,128]{2,1,0:T(8,128)(2,1)}), bf16[32,64,128]{2,1,0:T(8,128)(2,1)S(1)}, u32[]{:S(2)}, u32[]{:S(2)}) async-start(bf16[32,64,128]{2,1,0:T(8,128)(2,1)} %fusion.12), calls=%async_computation.2 | async-start | bytes 1048576 | tf_op jit(solution)/shard_map/all_to_all | solution.py:21
  117.0 39.9 %all-to-all-start.3 = ((bf16[32,320,128]{2,1,0:T(8,128)(2,1)}), bf16[32,320,128]{2,1,0:T(8,128)(2,1)}, u32[]{:S(2)}, u32[]{:S(2)}) async-start(bf16[32,320,128]{2,1,0:T(8,128)(2,1)} %broadcast_dynamic-update-slice_fusion), calls=%async_computation.3 | async-start | bytes 5242880 | tf_op jit(solution)/shard_map/all_to_all | solution.py:120
Sparse Core Ops, SparseCore 0:
  11.7 50.9 all-gather.1
where the time goes:
time: 170 us; the launch traced here: 169 us
  waiting for transfers between devices  74.3 us (44%)
  starting transfers between devices  26.1 us (15%)
  local copies, waits for them, and re-layouts  23.7 us (14%)
  matrix products  16.7 us (10%)
  between operations  14.9 us (9%)
  other arithmetic  12.7 us (7%)
    all_gather x1, waiting for transfers between devices, per_device(): lax.all_gather(packed, 'col', axis=0, tiled=True)  39.9 us
    all_to_all x1, waiting for transfers between devices, per_device(): incoming = lax.all_to_all(outgoing, 'row', 0, 0, tiled=True)  32.4 us
    all_to_all x2, starting transfers between devices, gather_rows(): got = lax.all_to_all(spread, axis_name, 0, 0, tiled=True)  12.8 us
    all_to_all x1, starting transfers between devices, reduce_rows(): got = lax.all_to_all(pieces, axis_name, 0, 0, tiled=True)  7.37 us
    reshape x1, local copies, waits for them, and re-layouts, per_device(): dense_t = jnp.transpose(dense, (0, 2, 4, 1, 3)).reshape(nodes, node_rows)  7.29 us
    all_to_all x1, starting transfers between devices, per_device(): incoming = lax.all_to_all(outgoing, 'row', 0, 0, tiled=True)  5.89 us
    dot_general x1, matrix products, per_device(): jnp.dot(dense_t, aggregated_grad, preferred_element_type=jnp.float32)  5.33 us
    broadcast_in_dim x2, local copies, waits for them, and re-layouts, gather_rows(): spread = jnp.broadcast_to(block[None], (parts,) + block.shape)  3.48 us
  transfers between devices with their start and end apart: 5, of which 4 were waited for; matrix products, arithmetic and copies ran while one was open for 19% of the time, Pallas kernels for 0%

commit v1 on v0

--- a/solution.py
+++ b/solution.py
@@ -3,6 +3,27 @@
 import jax.numpy as jnp
 from jax import lax
 from jax.sharding import PartitionSpec as P
+
+
+def lift_terms(mat, axis_tag, pos_dim):
+    spare, part_now, y_new = (lax.axis_size(axis_tag), lax.axis_index(axis_tag), mat.shape[pos_dim])
+    in_order = list(map(lambda i: (i, (i + 1) % spare), range(spare)))
+    buffers = list(map(lambda i: (i, (i - 1) % spare), range(spare)))
+    out_arr = jnp.zeros((*mat.shape[:pos_dim], spare * y_new, *mat.shape[pos_dim + 1 :]), mat.dtype)
+    high = clean = mat
+    out_arr = lax.dynamic_update_slice_in_dim(out_arr, mat, part_now * y_new, axis=pos_dim)
+    w_next = spare // 2
+    for b in range(1, w_next + 1):
+        high = lax.ppermute(high, axis_tag, in_order)
+        out_arr = lax.dynamic_update_slice_in_dim(
+            out_arr, high, (part_now - b) % spare * y_new, axis=pos_dim
+        )
+        if b < spare - w_next:
+            clean = lax.ppermute(clean, axis_tag, buffers)
+            out_arr = lax.dynamic_update_slice_in_dim(
+                out_arr, clean, (part_now + b) % spare * y_new, axis=pos_dim
+            )
+    return out_arr
 
 
 def silu_grad(preact):
@@ -36,9 +57,7 @@
         pos_row, positions[0, 0].astype(values.dtype).reshape(1, slots), (0, 0)
     )
     packed = jnp.concatenate([own_vals, pos_row, features, grad_out], axis=0)
-    all_packed = lax.all_gather(packed, "col", axis=0, tiled=True).reshape(
-        col_count, packed.shape[0], block_edge
-    )
+    all_packed = lift_terms(packed, "col", 0).reshape(col_count, packed.shape[0], block_edge)
     tile_vals = all_packed.reshape(col_count, -1, block_edge, block_edge)[:, :slots]
     tile_pos = all_packed[:, slots * block_edge, :slots].astype(jnp.int32)
     cb = row_count * node_rows // col_count // block_edge

time: 170 us -> 162 us (0.953)
  waiting for transfers between devices: 74.3 us -> 57 us
  starting transfers between devices: 26.1 us -> 42.1 us
  between operations: 14.9 us -> 1.8 us
  local copies, waits for them, and re-layouts: 23.7 us -> 30.4 us
    all_gather x1 -> x0, waiting for transfers between devices: 39.9 us -> none  [per_device(): lax.all_gather(packed, 'col', axis=0, tiled=True)]
    ppermute x0 -> x7, waiting for transfers between devices: none -> 23.1 us  [the longest x4 23 us: lift_terms(): high = lax.ppermute(high, axis_tag, in_order)]
    ppermute x0 -> x7, starting transfers between devices: none -> 11.8 us  [the longest x3 9.27 us: lift_terms(): clean = lax.ppermute(clean, axis_tag, buffers)]
    dynamic_update_slice x0 -> x7, local copies, waits for them, and re-layouts: none -> 5.56 us  [the longest x4 3.19 us: lift_terms(): lax.dynamic_update_slice_in_dim(out_arr, high, (part_now - b) % spare * y...]
    all_to_all x1, starting transfers between devices: 7.37 us -> 9.93 us  [reduce_rows(): got = lax.all_to_all(pieces, axis_name, 0, 0, tiled=True)]
    broadcast_in_dim x0 -> x1, local copies, waits for them, and re-layouts: none -> 1.93 us  [lift_terms(): jnp.zeros((*mat.shape[:pos_dim], spare * y_new, *mat.shape[pos_dim + 1:])...]
    all_to_all x2, starting transfers between devices: 12.8 us -> 14.5 us  [gather_rows(): got = lax.all_to_all(spread, axis_name, 0, 0, tiled=True)]
  transfers between devices with their start and end apart: 5 -> 11, of which waited for: 4 -> 5; matrix products, arithmetic and copies ran while one was open for 19% -> 23% of each run, Pallas kernels for 0% -> 0%
where the time goes in v1:
time: 162 us; the launch traced here: 161 us
  waiting for transfers between devices  57 us (35%)
  starting transfers between devices  42.1 us (26%)
  local copies, waits for them, and re-layouts  30.4 us (19%)
  matrix products  18.2 us (11%)
  other arithmetic  11.9 us (7%)
  between operations  1.8 us (1%)
    all_to_all x1, waiting for transfers between devices, per_device(): incoming = lax.all_to_all(outgoing, 'row', 0, 0, tiled=True)  32.4 us
    ppermute x4, waiting for transfers between devices, lift_terms(): high = lax.ppermute(high, axis_tag, in_order)  23 us
    all_to_all x2, starting transfers between devices, gather_rows(): got = lax.all_to_all(spread, axis_name, 0, 0, tiled=True)  14.5 us
    all_to_all x1, starting transfers between devices, reduce_rows(): got = lax.all_to_all(pieces, axis_name, 0, 0, tiled=True)  9.93 us
    ppermute x3, starting transfers between devices, lift_terms(): clean = lax.ppermute(clean, axis_tag, buffers)  9.27 us
    reshape x1, local copies, waits for them, and re-layouts, per_device(): dense_t = jnp.transpose(dense, (0, 2, 4, 1, 3)).reshape(nodes, node_rows)  7.31 us
    all_to_all x1, starting transfers between devices, per_device(): incoming = lax.all_to_all(outgoing, 'row', 0, 0, tiled=True)  5.89 us
    dot_general x1, matrix products, per_device(): jnp.dot(dense_t, aggregated_grad, preferred_element_type=jnp.float32)  5.33 us
  transfers between devices with their start and end apart: 11, of which 5 were waited for; matrix products, arithmetic and copies ran while one was open for 23% of the time, Pallas kernels for 0%

profile of v1, /device:TPU:1, one launch (start us, length us, event | category | flops | bytes accessed | tf_op | source)
XLA Modules:
  0.0 161.4 jit_solution(11887873867900331988)
XLA Ops:
  2.2 1.1 bitcast_multiply_fusion.1
  3.4 1.9 %broadcast_in_dim.8 = bf16[13312,128]{1,0:T(8,128)(2,1)} broadcast(bf16[]{:T(256)} %constant.78.clone.1), dimensions={} | broadcast | bytes 3407874 | tf_op jit(solution)/shard_map/broadcast_in_dim | solution.py:12
  5.3 1.0 fusion.17
  6.3 2.5 %collective-permute-start = (bf16[1664,128]{1,0:T(8,128)(2,1)}, bf16[1664,128]{1,0:T(8,128)(2,1)S(1)}, u32[]{:S(2)}, u32[]{:S(2)}) collective-permute-start(bf16[1664,128]{1,0:T(8,128)(2,1)} %get-tuple-element.16), channel_id=1, source_target_pairs={{0,1},{1,2},{2,3},{3,4},{4,5},{5,6},{6,7},{7,0},{8,9},{9,10},{10,1... | collective-permute-start | bytes 1277960 | tf_op jit(solution)/shard_map/ppermute | solution.py:17
  8.7 3.9 %collective-permute-start.1 = (bf16[1664,128]{1,0:T(8,128)(2,1)}, bf16[1664,128]{1,0:T(8,128)(2,1)S(1)}, u32[]{:S(2)}, u32[]{:S(2)}) collective-permute-start(bf16[1664,128]{1,0:T(8,128)(2,1)} %get-tuple-element.16), channel_id=1, source_target_pairs={{0,7},{1,0},{2,1},{3,2},{4,3},{5,4},{6,5},{7,6},{8,15},{9,8},{10,9... | collective-permute-start | bytes 1277960 | tf_op jit(solution)/shard_map/ppermute | solution.py:22
  12.6 1.8 %broadcast_in_dim.9 = bf16[32,256,128]{2,1,0:T(8,128)(2,1)} broadcast(bf16[256,128]{1,0:T(8,128)(2,1)S(1)} %copy-done.2), dimensions={1,2} | broadcast | bytes 2162688 | tf_op jit(solution)/shard_map/broadcast_in_dim | solution.py:35
  14.5 8.1 %all-to-all-start = ((bf16[32,256,128]{2,1,0:T(8,128)(2,1)}), bf16[32,256,128]{2,1,0:T(8,128)(2,1)}, u32[]{:S(2)}, u32[]{:S(2)}) async-start(bf16[32,256,128]{2,1,0:T(8,128)(2,1)} %broadcast_in_dim.9), calls=%async_computation | async-start | bytes 4194304 | tf_op jit(solution)/shard_map/all_to_all | solution.py:36
  22.8 2.7 %collective-permute-start.3 = (bf16[1664,128]{1,0:T(8,128)(2,1)S(1)}, bf16[1664,128]{1,0:T(8,128)(2,1)S(1)}, u32[]{:S(2)}, u32[]{:S(2)}) collective-permute-start(bf16[1664,128]{1,0:T(8,128)(2,1)S(1)} %collective-permute-done.1), channel_id=1, source_target_pairs={{0,7},{1,0},{2,1},{3,2},{4,3},{5,4},{6,5},{7,6},{8,15},{9,8},{10,9... | collective-permute-start | bytes 1277960 | tf_op jit(solution)/shard_map/ppermute | solution.py:22
  25.5 0.8 constant_dynamic-update-slice_fusion.6
  26.2 0.8 constant_dynamic-update-slice_fusion.5
  27.0 7.6 %collective-permute-done.2 = bf16[1664,128]{1,0:T(8,128)(2,1)S(1)} collective-permute-done((bf16[1664,128]{1,0:T(8,128)(2,1)S(1)}, bf16[1664,128]{1,0:T(8,128)(2,1)S(1)}, u32[]{:S(2)}, u32[]{:S(2)}) %collective-permute-start.2) | collective-permute-done | bytes 426016 | tf_op jit(solution)/shard_map/ppermute | solution.py:17
  34.6 2.7 %collective-permute-start.5 = (bf16[1664,128]{1,0:T(8,128)(2,1)S(1)}, bf16[1664,128]{1,0:T(8,128)(2,1)S(1)}, u32[]{:S(2)}, u32[]{:S(2)}) collective-permute-start(bf16[1664,128]{1,0:T(8,128)(2,1)S(1)} %collective-permute-done.3), channel_id=1, source_target_pairs={{0,7},{1,0},{2,1},{3,2},{4,3},{5,4},{6,5},{7,6},{8,15},{9,8},{10,9... | collective-permute-start | bytes 1277960 | tf_op jit(solution)/shard_map/ppermute | solution.py:22
  37.3 0.8 constant_dynamic-update-slice_fusion.4
  38.1 0.8 constant_dynamic-update-slice_fusion.3
  38.9 6.8 %collective-permute-done.4 = bf16[1664,128]{1,0:T(8,128)(2,1)S(1)} collective-permute-done((bf16[1664,128]{1,0:T(8,128)(2,1)S(1)}, bf16[1664,128]{1,0:T(8,128)(2,1)S(1)}, u32[]{:S(2)}, u32[]{:S(2)}) %collective-permute-start.4) | collective-permute-done | bytes 426016 | tf_op jit(solution)/shard_map/ppermute | solution.py:17
  45.7 0.8 constant_dynamic-update-slice_fusion.2
  46.5 0.8 constant_dynamic-update-slice_fusion.1
  47.3 8.6 %collective-permute-done.6 = bf16[1664,128]{1,0:T(8,128)(2,1)S(1)} collective-permute-done((bf16[1664,128]{1,0:T(8,128)(2,1)S(1)}, bf16[1664,128]{1,0:T(8,128)(2,1)S(1)}, u32[]{:S(2)}, u32[]{:S(2)}) %collective-permute-start.6) | collective-permute-done | bytes 426016 | tf_op jit(solution)/shard_map/ppermute | solution.py:17
  55.9 0.8 constant_dynamic-update-slice_fusion
  56.8 0.7 slice_convert_fusion.1
  57.6 2.9 %fusion.5 = bf16[8,8,128,128]{3,1,2,0:T(8,128)(2,1)S(1)} fusion(bf16[8,8,128,128]{3,2,1,0:T(8,128)(2,1)} %bitcast.9, s32[8,8]{1,0:T(8,128)S(1)} %get-tuple-element.18), kind=kOutput, calls=%fused_computation.10 | convolution fusion | flops 17826304 | bytes 4194560 | tf_op jit(solution)/shard_map/tsc,tcjf->tsjf/dot_general | solution.py:80
  60.5 2.3 %fusion.1 = f32[8,8,128,128]{3,2,1,0:T(8,128)S(1)} fusion(bf16[8,13,128,128]{3,2,1,0:T(8,128)(2,1)} %bitcast.4, bf16[8,8,128,128]{3,1,2,0:T(8,128)(2,1)S(1)} %fusion.5), kind=kOutput, calls=%fused_computation.6 | convolution fusion | flops 268435456 | bytes 9699328 | tf_op jit(solution)/shard_map/tsij,tsjf->tsif/dot_general | solution.py:83
  62.8 0.7 multiply_reduce_fusion
  63.7 0.8 broadcast_in_dim.10
  64.5 6.4 %all-to-all-start.1 = ((bf16[8,256,128]{1,2,0:T(8,128)(2,1)}), bf16[8,256,128]{1,2,0:T(8,128)(2,1)}, u32[]{:S(2)}, u32[]{:S(2)}) async-start(bf16[8,256,128]{1,2,0:T(8,128)(2,1)} %broadcast_in_dim.10), calls=%async_computation.1 | async-start | bytes 1048576 | tf_op jit(solution)/shard_map/all_to_all | solution.py:36
  70.9 1.3 slice.40
  72.2 1.8 %slice.39 = bf16[8,8,128,128]{3,2,1,0:T(8,128)(2,1)S(1)} slice(bf16[8,13,128,128]{3,2,1,0:T(8,128)(2,1)} %bitcast.4), slice={[0:8], [0:8], [0:128], [0:128]} | slice | bytes 4194304 | tf_op jit(solution)/shard_map/slice | solution.py:61
  74.0 0.7 copy.48
  74.7 1.9 %convert_bitcast_fusion = bf16[8,2,8,128,128]{4,2,1,3,0:T(8,128)(2,1)S(1)} fusion(bf16[8,8,128,128]{3,2,1,0:T(8,128)(2,1)S(1)} %slice.39, s32[8,8]{1,0:T(8,128)S(1)} %bitcast.92), kind=kOutput, calls=%fused_computation.4 | convolution fusion | flops 35652608 | bytes 6291712 | tf_op jit(solution)/shard_map/tsp,tsij->tpij/dot_general | solution.py:68
  76.6 3.2 %copy.47 = bf16[8,2,8,128,128]{4,2,0,3,1:T(8,128)(2,1)} copy(bf16[8,2,8,128,128]{4,2,1,3,0:T(8,128)(2,1)S(1)} %convert_bitcast_fusion) | data formatting | bytes 8388608 | tf_op jit(solution)/shard_map/reshape | solution.py:71
  79.8 7.3 %reshape.122 = bf16[8192,256]{0,1:T(8,128)(2,1)} reshape(bf16[8,8,128,2,128]{2,1,0,4,3:T(8,128)(2,1)} %bitcast.83) | data formatting | bytes 8388608 | tf_op jit(solution)/shard_map/reshape | solution.py:88
  87.1 1.3 slice_convert_fusion
  88.4 1.9 %fusion.34 = f32[256,1024]{1,0:T(8,128)S(1)} fusion(bf16[256,1024]{0,1:T(8,128)(2,1)} %bitcast.16, bf16[1024,1024]{1,0:T(8,128)(2,1)S(1)} %copy-done), kind=kOutput, calls=%fused_computation.70 | convolution fusion | flops 536870912 | bytes 3670016 | tf_op jit(solution)/shard_map/dot_general | solution.py:97
  90.6 2.1 %fusion.8 = (bf16[256,1024]{1,0:T(8,128)(2,1)S(1)}, f32[256,1024]{1,0:T(8,128)}) fusion(f32[32,8,8,128]{3,2,1,0:T(8,128)S(1)} %bitcast.87, f32[256,1024]{1,0:T(8,128)S(1)} %fusion.34, bf16[1024,1024]{1,0:T(8,128)(2,1)S(1)} %copy-done.5, bf16[32,8,8,128]{3,2,1,0:T(8,128)(2,1)S(1)} %bitcast.90), kind=kOutput, calls=%fused_computation.17 | convolution fusion | flops 539492352 | bytes 6291456 | tf_op jit(solution)/shard_map/dot_general | solution.py:97
  93.2 0.9 fusion.12
  94.2 9.9 %all-to-all-start.2 = ((bf16[32,64,128]{2,1,0:T(8,128)(2,1)}), bf16[32,64,128]{2,1,0:T(8,128)(2,1)S(1)}, u32[]{:S(2)}, u32[]{:S(2)}) async-start(bf16[32,64,128]{2,1,0:T(8,128)(2,1)} %fusion.12), calls=%async_computation.2 | async-start | bytes 1048576 | tf_op jit(solution)/shard_map/all_to_all | solution.py:42
  104.1 5.3 %convolution_convert_fusion = bf16[8192,128]{1,0:T(8,128)(2,1)} fusion(bf16[8192,256]{0,1:T(8,128)(2,1)} %reshape.122, bf16[256,1024]{1,0:T(8,128)(2,1)S(1)} %get-tuple-element.20, bf16[1024,1024]{1,0:T(8,128)(2,1)S(1)} %copy-done, s32[]{:T(128)S(6)} %select_n.96), kind=kOutput, calls=%fused_computation | convolution fusion | flops 605061120 | bytes 7077892 | tf_op jit(solution)/shard_map/dot_general | solution.py:131
  109.4 3.5 %concatenate.10 = bf16[32,320,128]{2,1,0:T(8,128)(2,1)} pad(bf16[32,256,128]{2,1,0:T(8,128)(2,1)} %bitcast.84, bf16[]{:T(256)} %constant.78.clone.1), padding=0_0x0_64x0_0 | pad | bytes 4718594 | tf_op jit(solution)/shard_map/concatenate | solution.py:134
  112.9 1.2 fusion.18
  114.2 1.6 all-to-all-done.2
  115.8 1.0 broadcast_dynamic-update-slice_fusion
  116.8 5.9 %all-to-all-start.3 = ((bf16[32,320,128]{2,1,0:T(8,128)(2,1)}), bf16[32,320,128]{2,1,0:T(8,128)(2,1)}, u32[]{:S(2)}, u32[]{:S(2)}) async-start(bf16[32,320,128]{2,1,0:T(8,128)(2,1)} %broadcast_dynamic-update-slice_fusion), calls=%async_computation.3 | async-start | bytes 5242880 | tf_op jit(solution)/shard_map/all_to_all | solution.py:139
  122.7 1.6 multiply_convert_fusion
  124.2 32.4 %all-to-all-done.3 = bf16[32,320,128]{2,1,0:T(8,128)(2,1)} async-done(((bf16[32,320,128]{2,1,0:T(8,128)(2,1)}), bf16[32,320,128]{2,1,0:T(8,128)(2,1)}, u32[]{:S(2)}, u32[]{:S(2)}) %all-to-all-start.3) | async-done | bytes 2621472 | tf_op jit(solution)/shard_map/all_to_all | solution.py:139
  156.6 1.1 convert_bitcast_fusion.1
  157.8 1.1 slice_bitcast_fusion
  158.9 1.9 %convert_reduce_fusion = f32[256,128]{1,0:T(8,128)S(1)} fusion(bf16[32,320,128]{2,1,0:T(8,128)(2,1)} %all-to-all-done.3), kind=kLoop, calls=%fused_computation.3 | loop fusion | flops 2064384 | bytes 2228224 | tf_op jit(solution)/shard_map/reduce_sum | solution.py:140
  160.8 0.7 add.123
  (30 shorter events, 1.9 us)
Async XLA Ops:
  0.6 87.8 %copy-start = (bf16[1024,1024]{1,0:T(8,128)(2,1)S(1)}, bf16[1024,1024]{1,0:T(8,128)(2,1)}, u32[]{:S(2)}) copy-start(bf16[1024,1024]{1,0:T(8,128)(2,1)} %param.9) | copy-start | bytes 6291460
  0.6 4.7 %copy-start.2 = (bf16[256,128]{1,0:T(8,128)(2,1)S(1)}, bf16[256,128]{1,0:T(8,128)(2,1)}, u32[]{:S(2)}) copy-start(bf16[256,128]{1,0:T(8,128)(2,1)} %param.7) | copy-start | bytes 196612
  0.7 4.6 %copy-start.4 = (bf16[256,128]{1,0:T(8,128)(2,1)S(1)}, bf16[256,128]{1,0:T(8,128)(2,1)}, u32[]{:S(2)}) copy-start(bf16[256,128]{1,0:T(8,128)(2,1)} %param.8) | copy-start | bytes 196612
  6.3 16.4 %collective-permute-start = (bf16[1664,128]{1,0:T(8,128)(2,1)}, bf16[1664,128]{1,0:T(8,128)(2,1)S(1)}, u32[]{:S(2)}, u32[]{:S(2)}) collective-permute-start(bf16[1664,128]{1,0:T(8,128)(2,1)} %get-tuple-element.16), channel_id=1, source_target_pairs={{0,1},{1,2},{2,3},{3,4},{4,5},{5,6},{6,7},{7,0},{8,9},{9,10},{10,1... | collective-permute-start | bytes 1277960 | tf_op jit(solution)/shard_map/ppermute | solution.py:17
  8.7 14.1 %collective-permute-start.1 = (bf16[1664,128]{1,0:T(8,128)(2,1)}, bf16[1664,128]{1,0:T(8,128)(2,1)S(1)}, u32[]{:S(2)}, u32[]{:S(2)}) collective-permute-start(bf16[1664,128]{1,0:T(8,128)(2,1)} %get-tuple-element.16), channel_id=1, source_target_pairs={{0,7},{1,0},{2,1},{3,2},{4,3},{5,4},{6,5},{7,6},{8,15},{9,8},{10,9... | collective-permute-start | bytes 1277960 | tf_op jit(solution)/shard_map/ppermute | solution.py:22
  14.5 43.1 %all-to-all-start = ((bf16[32,256,128]{2,1,0:T(8,128)(2,1)}), bf16[32,256,128]{2,1,0:T(8,128)(2,1)}, u32[]{:S(2)}, u32[]{:S(2)}) async-start(bf16[32,256,128]{2,1,0:T(8,128)(2,1)} %broadcast_in_dim.9), calls=%async_computation | async-start | bytes 4194304 | tf_op jit(solution)/shard_map/all_to_all | solution.py:36
  22.7 11.9 %collective-permute-start.2 = (bf16[1664,128]{1,0:T(8,128)(2,1)S(1)}, bf16[1664,128]{1,0:T(8,128)(2,1)S(1)}, u32[]{:S(2)}, u32[]{:S(2)}) collective-permute-start(bf16[1664,128]{1,0:T(8,128)(2,1)S(1)} %collective-permute-done), channel_id=1, source_target_pairs={{0,1},{1,2},{2,3},{3,4},{4,5},{5,6},{6,7},{7,0},{8,9},{9,10},{10,1... | collective-permute-start | bytes 1277960 | tf_op jit(solution)/shard_map/ppermute | solution.py:17
  22.8 11.8 %collective-permute-start.3 = (bf16[1664,128]{1,0:T(8,128)(2,1)S(1)}, bf16[1664,128]{1,0:T(8,128)(2,1)S(1)}, u32[]{:S(2)}, u32[]{:S(2)}) collective-permute-start(bf16[1664,128]{1,0:T(8,128)(2,1)S(1)} %collective-permute-done.1), channel_id=1, source_target_pairs={{0,7},{1,0},{2,1},{3,2},{4,3},{5,4},{6,5},{7,6},{8,15},{9,8},{10,9... | collective-permute-start | bytes 1277960 | tf_op jit(solution)/shard_map/ppermute | solution.py:22
  34.6 11.1 %collective-permute-start.4 = (bf16[1664,128]{1,0:T(8,128)(2,1)S(1)}, bf16[1664,128]{1,0:T(8,128)(2,1)S(1)}, u32[]{:S(2)}, u32[]{:S(2)}) collective-permute-start(bf16[1664,128]{1,0:T(8,128)(2,1)S(1)} %collective-permute-done.2), channel_id=1, source_target_pairs={{0,1},{1,2},{2,3},{3,4},{4,5},{5,6},{6,7},{7,0},{8,9},{9,10},{10,1... | collective-permute-start | bytes 1277960 | tf_op jit(solution)/shard_map/ppermute | solution.py:17
  34.6 11.9 %collective-permute-start.5 = (bf16[1664,128]{1,0:T(8,128)(2,1)S(1)}, bf16[1664,128]{1,0:T(8,128)(2,1)S(1)}, u32[]{:S(2)}, u32[]{:S(2)}) collective-permute-start(bf16[1664,128]{1,0:T(8,128)(2,1)S(1)} %collective-permute-done.3), channel_id=1, source_target_pairs={{0,7},{1,0},{2,1},{3,2},{4,3},{5,4},{6,5},{7,6},{8,15},{9,8},{10,9... | collective-permute-start | bytes 1277960 | tf_op jit(solution)/shard_map/ppermute | solution.py:22
  45.7 10.2 %collective-permute-start.6 = (bf16[1664,128]{1,0:T(8,128)(2,1)S(1)}, bf16[1664,128]{1,0:T(8,128)(2,1)S(1)}, u32[]{:S(2)}, u32[]{:S(2)}) collective-permute-start(bf16[1664,128]{1,0:T(8,128)(2,1)S(1)} %collective-permute-done.4), channel_id=1, source_target_pairs={{0,1},{1,2},{2,3},{3,4},{4,5},{5,6},{6,7},{7,0},{8,9},{9,10},{10,1... | collective-permute-start | bytes 1277960 | tf_op jit(solution)/shard_map/ppermute | solution.py:17
  64.5 23.9 %all-to-all-start.1 = ((bf16[8,256,128]{1,2,0:T(8,128)(2,1)}), bf16[8,256,128]{1,2,0:T(8,128)(2,1)}, u32[]{:S(2)}, u32[]{:S(2)}) async-start(bf16[8,256,128]{1,2,0:T(8,128)(2,1)} %broadcast_in_dim.10), calls=%async_computation.1 | async-start | bytes 1048576 | tf_op jit(solution)/shard_map/all_to_all | solution.py:36
  88.4 2.0 %copy-start.3 = (bf16[1,256,8,128]{3,2,1,0:T(8,128)(2,1)S(1)}, bf16[1,256,8,128]{3,2,1,0:T(8,128)(2,1)}, u32[]{:S(2)}) copy-start(bf16[1,256,8,128]{3,2,1,0:T(8,128)(2,1)} %get-tuple-element.15) | copy-start | bytes 1572868
  88.4 2.0 %copy-start.1 = (f32[1,256,8,128]{3,2,1,0:T(8,128)S(1)}, f32[1,256,8,128]{3,2,1,0:T(8,128)}, u32[]{:S(2)}) copy-start(f32[1,256,8,128]{3,2,1,0:T(8,128)} %get-tuple-element.14) | copy-start | bytes 3145732
  88.4 2.2 %copy-start.5 = (bf16[1024,1024]{1,0:T(8,128)(2,1)S(1)}, bf16[1024,1024]{1,0:T(8,128)(2,1)}, u32[]{:S(2)}) copy-start(bf16[1024,1024]{1,0:T(8,128)(2,1)} %param.10) | copy-start | bytes 6291460
  94.2 21.5 %all-to-all-start.2 = ((bf16[32,64,128]{2,1,0:T(8,128)(2,1)}), bf16[32,64,128]{2,1,0:T(8,128)(2,1)S(1)}, u32[]{:S(2)}, u32[]{:S(2)}) async-start(bf16[32,64,128]{2,1,0:T(8,128)(2,1)} %fusion.12), calls=%async_computation.2 | async-start | bytes 1048576 | tf_op jit(solution)/shard_map/all_to_all | solution.py:42
  116.8 39.9 %all-to-all-start.3 = ((bf16[32,320,128]{2,1,0:T(8,128)(2,1)}), bf16[32,320,128]{2,1,0:T(8,128)(2,1)}, u32[]{:S(2)}, u32[]{:S(2)}) async-start(bf16[32,320,128]{2,1,0:T(8,128)(2,1)} %broadcast_dynamic-update-slice_fusion), calls=%async_computation.3 | async-start | bytes 5242880 | tf_op jit(solution)/shard_map/all_to_all | solution.py:139
